TPU v7x, 256 devices: a whole 4x4x8 slice. The times are simulated.
256 devices in a mesh: seq: 16 (over x_lo, y, core), chan: 16 (over x_hi, z).
Axes of the slice: x: 4 (x_hi: 2, x_lo: 2; x = x_hi * 2 + x_lo), y: 4, z: 8, core: 2. Of those that a mesh axis runs over, the one named last changes fastest.
Arguments:
- tokens: int32 [4096], P('seq'), may hold values from 0 to 511
- embedding: bfloat16 [512, 4096], P(None, 'chan'), may hold values from -6 to 6
- norm_gain: float32 [4096], replicated, may hold values from 0.5 to 1.5
- in_weight: bfloat16 [4096, 3, 4096], P(None, None, 'chan'), may hold values from -0.09375 to 0.09375
- short_filter: float32 [3, 3, 4096], P(None, None, 'chan'), may hold values from -3 to 3
- decay_rate: float32 [16, 4096], P(None, 'chan'), may hold values from 4.8828125e-06 to 0.025, as said below
- residue: float32 [16, 4096], P(None, 'chan'), may hold values from -0.06 to 0.06
- skip_gain: float32 [4096], P('chan'), may hold values from -4 to 4
- out_weight: bfloat16 [4096, 4096], P('chan'), may hold values from -0.125 to 0.125
Outputs:
- block_out: bfloat16 [4096, 4096], P('seq', 'chan')
Inputs may be any that keep to these rules, and one draw needn't show every extreme that they name: `decay_rate`: positive rates.
All inputs are finite; a program needn't handle non-finite values.
Results may differ from a plain program's by a relative error of at most 0.0091.
Values may be sent and summed in bfloat16 or wider, within the bound.
No kernel may reach another device: no remote copies, remote signals or barrier semaphores. Data moves between devices by JAX's collectives and lax.ppermute only.
A program may use at most 128 MiB of HBM per device.

v0:
```python
import jax
import jax.numpy as jnp
from jax import lax
from jax.sharding import PartitionSpec as P

FEAT = 3


def from_behind(value, axis, by):
    devices = lax.axis_size(axis)
    pairs = [(i, i + by) for i in range(devices) if 0 <= i + by < devices]
    return lax.ppermute(value, axis, pairs)


def on_device(
    tokens,
    embedding,
    norm_gain,
    in_weight,
    short_filter,
    decay_rate,
    residue,
    skip_gain,
    out_weight,
):
    token_rows = tokens.shape[0]
    vocab_size = embedding.shape[0]
    channels = embedding.shape[1]
    modes = decay_rate.shape[0]
    seq_devices = lax.axis_size("seq")
    place = lax.axis_index("seq")
    weight_cols = lax.all_to_all(out_weight, "chan", 1, 0, tiled=True)
    one_hot = (tokens[:, None] == jnp.arange(vocab_size, dtype=jnp.int32)[None, :]).astype(
        jnp.bfloat16
    )
    stream = jnp.dot(one_hot, embedding, preferred_element_type=jnp.float32).astype(jnp.bfloat16)
    gathered = lax.all_gather(stream, "chan", axis=1, tiled=True)
    gathered_f = gathered.astype(jnp.float32)
    scale = lax.rsqrt(jnp.mean(gathered_f * gathered_f, axis=1, keepdims=True) + 1e-06)
    normed = (gathered_f * scale * norm_gain[None, :]).astype(jnp.bfloat16)
    proj = jnp.einsum("td,djc->tjc", normed, in_weight, preferred_element_type=jnp.float32).astype(
        jnp.bfloat16
    )
    rim_rows = FEAT - 1
    earlier_rim = from_behind(proj[token_rows - rim_rows :], "seq", 1)
    padded = jnp.concatenate([earlier_rim, proj], axis=0).astype(jnp.float32)
    feat = short_filter[0][None] * padded[rim_rows : rim_rows + token_rows]
    for offset in range(1, FEAT):
        feat = (
            feat
            + short_filter[offset][None]
            * padded[rim_rows - offset : rim_rows - offset + token_rows]
        )
    feat = feat.astype(jnp.bfloat16)
    query = feat[:, 0].astype(jnp.float32)
    driven = feat[:, 1].astype(jnp.float32) * feat[:, 2].astype(jnp.float32)
    pos = jnp.arange(token_rows, dtype=jnp.float32)
    rise = jnp.exp(decay_rate[None] * pos[:, None, None])
    fall = residue[None] * jnp.exp(-decay_rate[None] * pos[:, None, None])
    rows = jnp.arange(token_rows)
    lower = (rows[:, None] >= rows[None, :]).astype(jnp.float32)
    lifted = rise * driven[:, None, :]
    running = jnp.dot(
        lower, lifted.reshape(token_rows, modes * channels), precision=lax.Precision.HIGHEST
    ).reshape(token_rows, modes, channels)
    local = jnp.sum(fall * running, axis=1)
    device_end = jnp.exp(-decay_rate * (token_rows - 1)) * jnp.sum(lifted, axis=0)
    ends = lax.all_gather(device_end, "seq")
    gap = place - 1 - jnp.arange(seq_devices)
    span = jnp.exp(
        -decay_rate[None] * (token_rows * jnp.maximum(gap, 0)).astype(jnp.float32)[:, None, None]
    )
    span = jnp.where((gap >= 0)[:, None, None], span, 0.0)
    incoming = jnp.sum(span * ends, axis=0) * jnp.exp(-decay_rate)
    carried = jnp.sum(fall * incoming[None], axis=1)
    long_out = local + carried + skip_gain[None, :] * driven
    hidden = (query * long_out).astype(jnp.bfloat16)
    hidden_all = lax.all_gather(hidden, "chan", axis=1, tiled=True)
    mixed = jnp.dot(hidden_all, weight_cols, preferred_element_type=jnp.float32)
    return (stream.astype(jnp.float32) + mixed).astype(jnp.bfloat16)


def solution(mesh):
    placed = (
        P("seq"),
        P(None, "chan"),
        P(),
        P(None, None, "chan"),
        P(None, None, "chan"),
        P(None, "chan"),
        P(None, "chan"),
        P("chan"),
        P("chan", None),
    )
    return jax.shard_map(
        on_device, mesh=mesh, in_specs=placed, out_specs=P("seq", "chan"), check_vma=False
    )
```

profile of v0, /device:TPU:8, one launch (start us, length us, event | category | flops | bytes accessed | tf_op | source)
XLA Modules:
  0.0 251.8 jit_solution(8482166742746502454)
XLA Ops:
  6.5 0.9 copy-done
  7.5 1.6 convolution_convert_fusion
  9.1 0.0 all-gather.4.cloned.1.call-update
  9.1 0.0 copy-start.3
  9.1 4.1 %copy.11 = bf16[256,4096]{0,1:T(8,128)(2,1)} copy(bf16[256,4096]{1,0:T(8,128)(2,1)} %param.17) | data formatting | bytes 4194304 | tf_op args[8]
  13.2 11.2 %all-to-all-start = ((bf16[256,16,256]{0,2,1:T(8,128)(2,1)}), bf16[256,16,256]{0,2,1:T(8,128)(2,1)S(1)}, u32[]{:S(2)}, u32[]{:S(2)}) async-start(bf16[256,16,256]{0,2,1:T(8,128)(2,1)} %bitcast.40), calls=%async_computation | async-start | bytes 4194304 | tf_op jit(solution)/shard_map/all_to_all | solution.py:32
  24.4 0.0 all-gather.6.cloned.1.call-start
  24.5 97.7 %all-gather.4.cloned.1.call-done = bf16[256,4096]{1,0:T(8,128)(2,1)} async-done(((bf16[256,256]{1,0:T(8,128)(2,1)}), bf16[256,4096]{1,0:T(8,128)(2,1)}) %all-gather.4.cloned.1.call-update) | async-done | bytes 2097168 | tf_op jit(solution)/shard_map/all_gather | solution.py:37
  122.2 2.1 fusion
  124.3 0.0 copy-start.1
  124.3 5.3 %fusion.8 = bf16[256,3,256]{2,0,1:T(8,128)(2,1)S(1)} fusion(bf16[4096,3,256]{2,0,1:T(8,128)(2,1)} %param.12, bf16[256,4096]{1,0:T(8,128)(2,1)} %all-gather.4.cloned.1.call-done, f32[4096]{0:T(1024)S(1)} %copy-done.5, f32[256]{0:T(256)S(1)} %add_rsqrt_fusion), kind=kOutput, calls=%fused_computation.14 | convolution fusion | flops 1615003648 | bytes 8799232 | tf_op jit(solution)/shard_map/td,djc->tjc/dot_general | solution.py:41
  129.6 1.9 collective-permute-start
  131.5 2.9 %collective-permute-done = bf16[2,3,256]{2,0,1:T(2,128)(2,1)S(1)} collective-permute-done((bf16[2,3,256]{2,0,1:T(2,128)(2,1)S(1)}, bf16[2,3,256]{2,0,1:T(2,128)(2,1)S(1)}, u32[]{:S(2)}, u32[]{:S(2)}) %collective-permute-start) | collective-permute-done | bytes 3104 | tf_op jit(solution)/shard_map/ppermute | solution.py:12
  134.5 0.1 maximum_convert_fusion
  134.6 0.3 fusion.13
  134.8 0.0 copy-start.6
  134.9 0.1 copy.10
  135.0 1.3 multiply_reduce_fusion.1
  136.4 16.6 %all-gather = f32[256,256]{1,0:T(8,128)S(1)} all-gather(f32[16,256]{1,0:T(8,128)S(1)} %get-tuple-element.5), channel_id=2, replica_groups=mesh['seq'=16,'chan'=16] {'seq'}, dimensions={0}, use_global_device_ids=true | all-gather | bytes 278528 | tf_op jit(solution)/shard_map/all_gather | solution.py:68
  153.0 0.1 multiply_reduce_fusion.3
  153.1 0.6 bitcast_multiply_fusion
  153.8 0.0 copy-start.4
  153.8 0.9 multiply_reduce_fusion
  154.7 3.3 %multiply_reduce_fusion.2 = f32[256,256]{1,0:T(8,128)S(1)} fusion(f32[16,256,256]{2,1,0:T(8,128)S(1)} %bitcast.41, f32[16,256]{1,0:T(8,128)S(1)} %get-tuple-element.6, f32[16,256]{1,0:T(8,128)S(1)} %copy-done.6), kind=kOutput, calls=%fused_computation.8 | convolution fusion | flops 3225419776 | bytes 4489216 | tf_op jit(solution)/shard_map/dot_general | solution.py:63
  157.9 0.0 copy-done.4
  157.9 0.0 copy-start.2
  157.9 0.7 fusion.15
  158.7 0.0 all-gather.6.cloned.1.call-update
  158.7 0.0 all-to-all-done
  158.7 2.4 copy.12
  161.1 80.3 %all-gather.6.cloned.1.call-done = bf16[256,4096]{1,0:T(8,128)(2,1)} async-done(((bf16[256,256]{1,0:T(8,128)(2,1)}), bf16[256,4096]{1,0:T(8,128)(2,1)}) %all-gather.6.cloned.1.call-update) | async-done | bytes 2097168 | tf_op jit(solution)/shard_map/all_gather | solution.py:78
  241.4 3.6 %fusion.11 = bf16[256,256]{1,0:T(8,128)(2,1)} fusion(bf16[256,4096]{1,0:T(8,128)(2,1)} %all-gather.6.cloned.1.call-done, bf16[4096,256]{1,0:T(8,128)(2,1)} %bitcast.42, bf16[256,256]{1,0:T(8,128)(2,1)S(1)} %copy-done.2), kind=kOutput, calls=%fused_computation.16 | convolution fusion | flops 537067520 | bytes 4456448 | tf_op jit(solution)/shard_map/dot_general | solution.py:79
  (17 shorter events, 0.1 us)
Async XLA Ops:
  6.5 1.0 copy-start
  6.5 115.6 %all-gather.4.cloned.1.call-start = ((), (), s32[]{:S(2)}) async-start(), calls=%async_computation.1 | async-start | bytes 2228224 | tf_op jit(solution)/shard_map/all_gather | solution.py:37
  9.1 15.3 %copy-start.3 = (f32[3,3,256]{2,1,0:T(4,128)S(1)}, f32[3,3,256]{2,1,0:T(4,128)}, u32[]{:S(2)}) copy-start(f32[3,3,256]{2,1,0:T(4,128)} %param.13) | copy-start | bytes 27652
  13.2 111.0 %copy-start.5 = (f32[4096]{0:T(1024)S(1)}, f32[4096]{0:T(1024)}, u32[]{:S(2)}) copy-start(f32[4096]{0:T(1024)} %param.11) | copy-start | bytes 49156
  13.2 145.5 %all-to-all-start = ((bf16[256,16,256]{0,2,1:T(8,128)(2,1)}), bf16[256,16,256]{0,2,1:T(8,128)(2,1)S(1)}, u32[]{:S(2)}, u32[]{:S(2)}) async-start(bf16[256,16,256]{0,2,1:T(8,128)(2,1)} %bitcast.40), calls=%async_computation | async-start | bytes 4194304 | tf_op jit(solution)/shard_map/all_to_all | solution.py:32
  24.4 217.0 %all-gather.6.cloned.1.call-start = ((), (), s32[]{:S(2)}) async-start(), calls=%async_computation.2 | async-start | bytes 2228224 | tf_op jit(solution)/shard_map/all_gather | solution.py:78
  124.3 7.3 %copy-start.1 = (f32[16,256]{1,0:T(8,128)S(1)}, f32[16,256]{1,0:T(8,128)}, u32[]{:S(2)}) copy-start(f32[16,256]{1,0:T(8,128)} %param.14) | copy-start | bytes 49156
  129.6 4.9 %collective-permute-start = (bf16[2,3,256]{2,0,1:T(2,128)(2,1)S(1)}, bf16[2,3,256]{2,0,1:T(2,128)(2,1)S(1)}, u32[]{:S(2)}, u32[]{:S(2)}) collective-permute-start(bf16[2,3,256]{2,0,1:T(2,128)(2,1)S(1)} %slice.40), channel_id=1, source_target_pairs={{0,16},{16,32},{32,48},{48,64},{64,80},{80,96},{96,112},{112,128},... | collective-permute-start | bytes 9224 | tf_op jit(solution)/shard_map/ppermute | solution.py:12
  134.8 18.9 %copy-start.6 = (f32[16,256]{1,0:T(8,128)S(1)}, f32[16,256]{1,0:T(8,128)}, u32[]{:S(2)}) copy-start(f32[16,256]{1,0:T(8,128)} %param.15) | copy-start | bytes 49156
  153.8 4.2 %copy-start.4 = (f32[256]{0:T(256)S(1)}, f32[256]{0:T(256)}, u32[]{:S(2)}) copy-start(f32[256]{0:T(256)} %param.16) | copy-start | bytes 3076
  157.9 83.5 %copy-start.2 = (bf16[256,256]{1,0:T(8,128)(2,1)S(1)}, bf16[256,256]{1,0:T(8,128)(2,1)}, u32[]{:S(2)}) copy-start(bf16[256,256]{1,0:T(8,128)(2,1)} %convolution_convert_fusion) | copy-start | bytes 393220
Sparse Core Ops, SparseCore 0:
  9.8 112.3 all-gather.3
  158.8 82.5 all-gather.5
where the time goes:
time: 252 us
  waiting for transfers between devices  181 us (72%)
  blocking collectives  16.6 us (7%)
  matrix products  13.7 us (5%)
  between operations  13.6 us (5%)
  starting transfers between devices  13.1 us (5%)
  local copies, waits for them, and re-layouts  7.62 us (3%)
  other arithmetic  6.17 us (2%)
    all_gather x1, waiting for transfers between devices, on_device(): gathered = lax.all_gather(stream, 'chan', axis=1, tiled=True)  97.7 us
    all_gather x1, waiting for transfers between devices, on_device(): hidden_all = lax.all_gather(hidden, 'chan', axis=1, tiled=True)  80.3 us
    all_gather x1, blocking collectives, on_device(): ends = lax.all_gather(device_end, 'seq')  16.6 us
    all_to_all x1, starting transfers between devices, on_device(): weight_cols = lax.all_to_all(out_weight, 'chan', 1, 0, tiled=True)  11.2 us
    dot_general x1, matrix products, on_device(): jnp.einsum('td,djc->tjc', normed, in_weight, preferred_element_type=jnp.f...  5.27 us
    unnamed x16, local copies, waits for them, and re-layouts  5.08 us
  transfers between devices with their start and end apart: 4, of which 3 were waited for; matrix products, arithmetic and copies ran while one was open for 8% of the time, Pallas kernels for 0%

commit v1 on v0

--- a/solution.py
+++ b/solution.py
@@ -75,7 +75,9 @@
     carried = jnp.sum(fall * incoming[None], axis=1)
     long_out = local + carried + skip_gain[None, :] * driven
     hidden = (query * long_out).astype(jnp.bfloat16)
-    hidden_all = lax.all_gather(hidden, "chan", axis=1, tiled=True)
+    hidden_all = jnp.concatenate(
+        lax.all_to_all(jnp.stack([hidden] * lax.axis_size("chan")), "chan", 0, 0), axis=1
+    )
     mixed = jnp.dot(hidden_all, weight_cols, preferred_element_type=jnp.float32)
     return (stream.astype(jnp.float32) + mixed).astype(jnp.bfloat16)
 

time: 252 us -> 238 us (0.944)
  waiting for transfers between devices: 181 us -> 100 us
  blocking collectives: 16.6 us -> 73.7 us
  local copies, waits for them, and re-layouts: 7.62 us -> 16.6 us
    all_gather x1 -> x0, waiting for transfers between devices: 80.3 us -> none  [on_device(): hidden_all = lax.all_gather(hidden, 'chan', axis=1, tiled=True)]
    all_to_all x0 -> x1, blocking collectives: none -> 56.8 us  [on_device(): lax.all_to_all(jnp.stack([hidden] * lax.axis_size('chan')), 'chan', 0, 0)]
    dot_general x0 -> x1, local copies, waits for them, and re-layouts: none -> 5.61 us  [on_device(): jnp.dot(lower, lifted.reshape(token_rows, modes * channels), precision=la...]
    unnamed x16 -> x19, local copies, waits for them, and re-layouts: 5.08 us -> 8.06 us
    dot_general x0 -> x1, other arithmetic: none -> 2.73 us  [on_device(): jnp.dot(lower, lifted.reshape(token_rows, modes * channels), precision=la...]
  transfers between devices with their start and end apart: 4 -> 3, of which waited for: 3 -> 2; matrix products, arithmetic and copies ran while one was open for 8% -> 13% of each run, Pallas kernels for 0% -> 0%
where the time goes in v1:
time: 238 us; the launch traced here: 236 us
  waiting for transfers between devices  100 us (42%)
  blocking collectives  73.7 us (31%)
  local copies, waits for them, and re-layouts  16.6 us (7%)
  between operations  13.6 us (6%)
  starting transfers between devices  13.1 us (6%)
  matrix products  11.5 us (5%)
  other arithmetic  7.02 us (3%)
    all_gather x1, waiting for transfers between devices, on_device(): gathered = lax.all_gather(stream, 'chan', axis=1, tiled=True)  97.3 us
    all_to_all x1, blocking collectives, on_device(): lax.all_to_all(jnp.stack([hidden] * lax.axis_size('chan')), 'chan', 0, 0)  56.8 us
    all_gather x1, blocking collectives, on_device(): ends = lax.all_gather(device_end, 'seq')  16.9 us
    all_to_all x1, starting transfers between devices, on_device(): weight_cols = lax.all_to_all(out_weight, 'chan', 1, 0, tiled=True)  11.2 us
    unnamed x19, local copies, waits for them, and re-layouts  8.06 us
    dot_general x1, local copies, waits for them, and re-layouts, on_device(): jnp.dot(lower, lifted.reshape(token_rows, modes * channels), precision=la...  5.61 us
    dot_general x1, matrix products, on_device(): jnp.einsum('td,djc->tjc', normed, in_weight, preferred_element_type=jnp.f...  5.27 us
  transfers between devices with their start and end apart: 3, of which 2 were waited for; matrix products, arithmetic and copies ran while one was open for 13% of the time, Pallas kernels for 0%

profile of v1, /device:TPU:8, one launch (start us, length us, event | category | flops | bytes accessed | tf_op | source)
XLA Modules:
  0.0 235.9 jit_solution(4212927493994398202)
XLA Ops:
  6.5 0.0 copy-start
  6.5 0.9 copy-done
  7.5 1.6 convolution_convert_fusion
  9.1 0.0 all-gather.3.cloned.1.call-update
  9.1 3.3 %copy.15 = bf16[256,4096]{0,1:T(8,128)(2,1)S(1)} copy(bf16[256,4096]{1,0:T(8,128)(2,1)} %param.17) | data formatting | bytes 4194304 | tf_op args[8]
  12.4 0.0 copy-start.4
  12.4 2.4 %copy.16 = bf16[256,16,256]{2,0,1:T(8,128)(2,1)} copy(bf16[256,16,256]{0,2,1:T(8,128)(2,1)S(1)} %bitcast.61) | data formatting | bytes 4194304 | tf_op jit(solution)/shard_map/all_to_all | solution.py:32
  14.8 11.2 %all-to-all-start.1 = ((bf16[256,16,256]{2,0,1:T(8,128)(2,1)}), bf16[256,16,256]{2,0,1:T(8,128)(2,1)S(1)}, u32[]{:S(2)}, u32[]{:S(2)}) async-start(bf16[256,16,256]{2,0,1:T(8,128)(2,1)} %copy.16), calls=%async_computation.1 | async-start | bytes 4194304 | tf_op jit(solution)/shard_map/all_to_all | solution.py:32
  26.1 97.3 %all-gather.3.cloned.1.call-done = bf16[256,4096]{1,0:T(8,128)(2,1)} async-done(((bf16[256,256]{1,0:T(8,128)(2,1)}), bf16[256,4096]{1,0:T(8,128)(2,1)}) %all-gather.3.cloned.1.call-update) | async-done | bytes 2097168 | tf_op jit(solution)/shard_map/all_gather | solution.py:37
  123.3 2.1 fusion
  125.4 0.0 copy-start.2
  125.4 5.3 %fusion.11 = bf16[256,3,256]{2,0,1:T(8,128)(2,1)S(1)} fusion(bf16[4096,3,256]{2,0,1:T(8,128)(2,1)} %param.12, bf16[256,4096]{1,0:T(8,128)(2,1)} %all-gather.3.cloned.1.call-done, f32[4096]{0:T(1024)S(1)} %copy-done.6, f32[256]{0:T(256)S(1)} %add_rsqrt_fusion), kind=kOutput, calls=%fused_computation.17 | convolution fusion | flops 1615003648 | bytes 8799232 | tf_op jit(solution)/shard_map/td,djc->tjc/dot_general | solution.py:41
  130.7 1.9 collective-permute-start
  132.7 2.9 %collective-permute-done = bf16[2,3,256]{2,0,1:T(2,128)(2,1)S(1)} collective-permute-done((bf16[2,3,256]{2,0,1:T(2,128)(2,1)S(1)}, bf16[2,3,256]{2,0,1:T(2,128)(2,1)S(1)}, u32[]{:S(2)}, u32[]{:S(2)}) %collective-permute-start) | collective-permute-done | bytes 3104 | tf_op jit(solution)/shard_map/ppermute | solution.py:12
  135.6 0.1 maximum_convert_fusion
  135.7 0.3 fusion.30
  136.0 0.3 mul.200
  136.4 3.8 %copy.20 = f32[32,8,16,256]{3,1,2,0:T(8,128)S(1)} copy(f32[32,8,16,256]{3,2,1,0:T(8,128)S(1)} %bitcast.60) | data formatting | bytes 8388608
  140.2 2.7 %multiply_bitcast_fusion = f32[4096,256]{0,1:T(8,128)} fusion(f32[256,4096]{1,0:T(8,128)S(1)} %bitcast.59, f32[4096]{0:T(1024)S(1)} %bitcast.65), kind=kLoop, calls=%fused_computation.8 | loop fusion | flops 2097152 | bytes 8404992 | tf_op jit(solution)/shard_map/dot_general | solution.py:63
  142.9 5.6 %copy.12 = f32[4096,256]{1,0:T(8,128)} copy(f32[4096,256]{0,1:T(8,128)} %multiply_bitcast_fusion) | data formatting | bytes 8388608 | tf_op jit(solution)/shard_map/dot_general | solution.py:63
  148.5 0.7 multiply_reduce_fusion.1
  149.3 16.9 %all-gather = f32[256,256]{1,0:T(8,128)S(1)} all-gather(f32[16,256]{1,0:T(8,128)S(1)} %get-tuple-element.5), channel_id=2, replica_groups=mesh['seq'=16,'chan'=16] {'seq'}, dimensions={0}, use_global_device_ids=true | all-gather | bytes 278528 | tf_op jit(solution)/shard_map/all_gather | solution.py:68
  166.2 0.1 multiply_reduce_fusion.3
  166.4 0.9 multiply_reduce_fusion
  167.2 0.0 copy-done.1
  167.2 3.3 %multiply_reduce_fusion.2 = f32[256,256]{1,0:T(8,128)S(1)} fusion(f32[16,256,256]{2,1,0:T(8,128)S(1)} %bitcast.62, f32[16,256]{1,0:T(8,128)S(1)} %get-tuple-element.6, f32[16,256]{1,0:T(8,128)S(1)} %copy-done.7), kind=kOutput, calls=%fused_computation.7 | convolution fusion | flops 3225419776 | bytes 4489216 | tf_op jit(solution)/shard_map/dot_general | solution.py:63
  170.5 0.0 copy-start.3
  170.5 0.1 fusion.32
  170.6 0.0 all-to-all-done.1
  170.6 0.2 stack.2
  170.8 56.8 %all_to_all.21 = bf16[16,256,256]{2,1,0:T(8,128)(2,1)S(1)} all-to-all(bf16[16,256,256]{2,1,0:T(8,128)(2,1)S(1)} %stack.2), channel_id=1, replica_groups=mesh['seq'=16,'chan'=16] {'chan'}, dimensions={0} | all-to-all | bytes 4194304 | tf_op jit(solution)/shard_map/all_to_all | solution.py:79
  227.6 1.4 fusion.24
  (20 shorter events, 0.1 us)
Async XLA Ops:
  6.5 1.0 copy-start
  6.5 116.8 %all-gather.3.cloned.1.call-start = ((), (), s32[]{:S(2)}) async-start(), calls=%async_computation.2 | async-start | bytes 2228224 | tf_op jit(solution)/shard_map/all_gather | solution.py:37
  12.4 13.6 %copy-start.4 = (f32[3,3,256]{2,1,0:T(4,128)S(1)}, f32[3,3,256]{2,1,0:T(4,128)}, u32[]{:S(2)}) copy-start(f32[3,3,256]{2,1,0:T(4,128)} %param.13) | copy-start | bytes 27652
  14.8 110.6 %copy-start.6 = (f32[4096]{0:T(1024)S(1)}, f32[4096]{0:T(1024)}, u32[]{:S(2)}) copy-start(f32[4096]{0:T(1024)} %param.11) | copy-start | bytes 49156
  14.8 155.8 %all-to-all-start.1 = ((bf16[256,16,256]{2,0,1:T(8,128)(2,1)}), bf16[256,16,256]{2,0,1:T(8,128)(2,1)S(1)}, u32[]{:S(2)}, u32[]{:S(2)}) async-start(bf16[256,16,256]{2,0,1:T(8,128)(2,1)} %copy.16), calls=%async_computation.1 | async-start | bytes 4194304 | tf_op jit(solution)/shard_map/all_to_all | solution.py:32
  125.4 7.3 %copy-start.2 = (f32[16,256]{1,0:T(8,128)S(1)}, f32[16,256]{1,0:T(8,128)}, u32[]{:S(2)}) copy-start(f32[16,256]{1,0:T(8,128)} %param.14) | copy-start | bytes 49156
  130.7 4.9 %collective-permute-start = (bf16[2,3,256]{2,0,1:T(2,128)(2,1)S(1)}, bf16[2,3,256]{2,0,1:T(2,128)(2,1)S(1)}, u32[]{:S(2)}, u32[]{:S(2)}) collective-permute-start(bf16[2,3,256]{2,0,1:T(2,128)(2,1)S(1)} %slice.40), channel_id=1, source_target_pairs={{0,16},{16,32},{32,48},{48,64},{64,80},{80,96},{96,112},{112,128},... | collective-permute-start | bytes 9224 | tf_op jit(solution)/shard_map/ppermute | solution.py:12
  142.9 23.4 %copy-start.7 = (f32[16,256]{1,0:T(8,128)S(1)}, f32[16,256]{1,0:T(8,128)}, u32[]{:S(2)}) copy-start(f32[16,256]{1,0:T(8,128)} %param.15) | copy-start | bytes 49156
  148.5 18.7 %copy-start.1 = (f32[4096,256]{1,0:T(8,128)S(1)}, f32[4096,256]{1,0:T(8,128)}, u32[]{:S(2)}) copy-start(f32[4096,256]{1,0:T(8,128)} %copy.12) | copy-start | bytes 12582916
  166.2 4.3 %copy-start.5 = (f32[256]{0:T(256)S(1)}, f32[256]{0:T(256)}, u32[]{:S(2)}) copy-start(f32[256]{0:T(256)} %param.16) | copy-start | bytes 3076
  170.5 57.1 %copy-start.3 = (bf16[256,256]{1,0:T(8,128)(2,1)S(1)}, bf16[256,256]{1,0:T(8,128)(2,1)}, u32[]{:S(2)}) copy-start(bf16[256,256]{1,0:T(8,128)(2,1)} %convolution_convert_fusion) | copy-start | bytes 393220
Sparse Core Ops, SparseCore 0:
  9.8 113.4 all-gather.2
